TPU v7x, 32 devices: a whole 2x2x4 slice. The times are simulated.
32 devices in a mesh: gx: 8 (over y, x, core), gy: 4 (over z).
Axes of the slice: x: 2, y: 2, z: 4, core: 2. Of those that a mesh axis runs over, the one named last changes fastest.
Arguments:
- temp_start: float32 [8, 1024, 2048], P(None, ('gx', 'gy')), may hold values from -6 to 6
- heat_input: float32 [8, 1024, 2048], P(None, ('gx', 'gy')), may hold values from -3 to 3
- lateral: float32 [8], replicated, may hold values from 0.03 to 0.15
- vertical: float32 [7], replicated, may hold values from 0.03 to 0.15
- weighting: float32 [8], replicated, may hold values from -1 to 1
- modulus: float32 [1024, 2048], P('gx', 'gy'), may hold values from 0.3 to 3
- warp_prev: float32 [1024, 2048], P('gx', 'gy'), may hold values from -6 to 6
- joint_cell: int32 [65536], P(('gx', 'gy')), may hold values from 0 to 65535
- joint_owner: int32 [65536, 1], P(('gx', 'gy')), may hold values from 0 to 31; in each aligned block of 2048 rows (0 to 2047, 2048 to 4095, ...) at most 192 rows name the same one
- joint_strain: float32 [2, 32, 6144], P(None, ('gx', 'gy')), may hold values from -4 to 4
- joint_resist: float32 [32, 6144], P(('gx', 'gy')), may hold values from 1 to 2
Outputs:
- warpage: float32 [1024, 2048], P('gx', 'gy')
- strain_next: float32 [2, 32, 6144], P(None, ('gx', 'gy'))
- resist_next: float32 [32, 6144], P(('gx', 'gy'))
Inputs may be any that keep to these rules, and one draw needn't show every extreme that they name: `joint_owner`: among the 2048 joints of one device at most 192 have the same owner, and on some device exactly 192 do.
All inputs are finite; a program needn't handle non-finite values.
Results may differ from a plain program's by a relative error of at most 0.0003.
Values sent between devices are 32-bit elements; how exact they have to be, the bound alone decides.
No kernel may reach another device: no remote copies, remote signals or barrier semaphores. Data moves between devices by JAX's collectives and lax.ppermute only.
A program may use at most 320 MiB of HBM per device.

v0:
```python
import jax
import jax.numpy as jnp
from jax import lax
from jax.sharding import PartitionSpec as P

STEPS = 2
SWEEPS = 3
stiffness = 0.2
shear_mod = 0.6
rate_scale = 0.5
sat_level = 2.5
sat_power = 0.3
harden = 2.0
FLAT = ("gx", "gy")


def exchange(last, leading, axis):
    count = lax.axis_size(axis)
    up = [(i, i + 1) for i in range(count - 1)]
    down = [(j, i) for i, j in up]
    return (lax.ppermute(last, axis, up), lax.ppermute(leading, axis, down))


def with_halo(array, sides, width):
    for axis, dim in sides:
        length = array.shape[dim]
        last = lax.slice_in_dim(array, length - width, length, axis=dim)
        leading = lax.slice_in_dim(array, 0, width, axis=dim)
        before, after = exchange(last, leading, axis)
        array = jnp.concatenate([before, array, after], axis=dim)
    return array


def thermal_step(ext, heat_rows, lateral, vertical):
    cols = jnp.pad(ext, ((0, 0), (0, 0), (1, 1)))
    center = ext[:, 1:-1]
    lap = ext[:, 2:] + ext[:, :-2] + cols[:, 1:-1, 2:] + cols[:, 1:-1, :-2] - 4.0 * center
    flux = vertical[:, None, None] * (center[1:] - center[:-1])
    vert = jnp.pad(flux, ((0, 1), (0, 0), (0, 0))) - jnp.pad(flux, ((1, 0), (0, 0), (0, 0)))
    return center + lateral[:, None, None] * lap + vert + heat_rows


def moment_of(field, weighting):
    total = weighting[0] * field[0]
    for layer in range(1, field.shape[0]):
        total = total + weighting[layer] * field[layer]
    return total


def sweep(w_pad, e_pad, load):
    center = e_pad[1:-1, 1:-1]
    e_up = 0.5 * (center + e_pad[:-2, 1:-1])
    e_down = 0.5 * (center + e_pad[2:, 1:-1])
    e_left = 0.5 * (center + e_pad[1:-1, :-2])
    e_right = 0.5 * (center + e_pad[1:-1, 2:])
    numer = (
        load
        + e_up * w_pad[:-2, 1:-1]
        + e_down * w_pad[2:, 1:-1]
        + e_left * w_pad[1:-1, :-2]
        + e_right * w_pad[1:-1, 2:]
    )
    denom = stiffness + e_up + e_down + e_left + e_right
    return numer / denom


def anand(strain, resist, recv):
    total, inelastic = (strain[0], strain[1])
    increment, theta, live = (recv[0], recv[1], recv[2])
    total_new = total + increment
    arrhen = jnp.exp(2.0 - 2.0 / (1.0 + 0.1 * theta * theta))
    hyper = jnp.sinh(shear_mod * (total_new - inelastic) / resist)
    rate = rate_scale * arrhen * hyper * jnp.abs(hyper)
    inelastic_new = inelastic + rate
    target = sat_level * jnp.power(1.0 + jnp.abs(rate) / arrhen, sat_power)
    resist_new = resist + harden * (1.0 - resist / target) * jnp.abs(rate)
    keep = live > 0.5
    strain_out = jnp.stack(
        [jnp.where(keep, total_new, total), jnp.where(keep, inelastic_new, inelastic)]
    )
    return (strain_out, jnp.where(keep, resist_new, resist))


def thermal(temp, heat, lateral, vertical):
    devices = lax.axis_size(FLAT)
    t = lax.axis_index(FLAT)
    rows = temp.shape[1]
    h = STEPS
    last = jnp.concatenate([temp[:, rows - h :], heat[:, rows - (h - 1) :]], axis=1)
    leading = jnp.concatenate([temp[:, :h], heat[:, : h - 1]], axis=1)
    before, after = exchange(last, leading, FLAT)
    ext = jnp.concatenate([before[:, :h], temp, after[:, :h]], axis=1)
    heat_ext = jnp.concatenate([before[:, h:], heat, after[:, h:]], axis=1)
    for step in range(1, STEPS + 1):
        r = STEPS - step
        heat_rows = heat_ext[:, h - 1 - r : h - 1 - r + rows + 2 * r]
        ext = thermal_step(ext, heat_rows, lateral, vertical)
        if r > 0:
            g = t * rows + jnp.arange(-r, rows + r)
            inside = (g >= 0) & (g < devices * rows)
            ext = jnp.where(inside[None, :, None], ext, 0.0)
    return ext


def relay(load, top, width):
    n_gy = lax.axis_size("gy")
    rows, cols = load.shape
    cm = cols // n_gy
    before, after = exchange(load[rows - width :], load[:width], FLAT)
    load_ext = jnp.concatenate([before, load, after], axis=0)
    lp = jnp.pad(load_ext, ((0, 0), (width, width)))
    tp = jnp.pad(top, ((width, width), (width, width)))
    both = jnp.stack([lp, tp])
    send = jnp.stack([both[:, :, k * cm : k * cm + cm + 2 * width] for k in range(n_gy)])
    recv = lax.all_to_all(send, "gy", split_axis=0, concat_axis=0, tiled=True)
    parts = []
    for k in range(n_gy):
        lo = 0 if k == 0 else width
        hi = rows + 2 * width if k == n_gy - 1 else rows + width
        parts.append(recv[k, 0, lo:hi])
    load_m = jnp.concatenate(parts, axis=0)
    top_m = jnp.concatenate(
        [recv[k, 1, width : rows + width, width : cm + width] for k in range(n_gy)], axis=0
    )
    return (load_m, top_m)


def joint_ranks(owners, devices):
    count = owners.shape[0]
    block = 128 if count % 128 == 0 else count
    nb = count // block
    onehot = (owners[:, None] == jnp.arange(devices, dtype=jnp.int32)[None, :]).astype(jnp.float32)
    oh = onehot.reshape(nb, block, devices)
    ar = jnp.arange(block)
    tri = (ar[:, None] >= ar[None, :]).astype(jnp.float32)
    within = jnp.einsum("ij,bjd->bid", tri, oh, precision=lax.Precision.HIGHEST)
    totals = within[:, -1, :]
    ab = jnp.arange(nb)
    stri = (ab[:, None] > ab[None, :]).astype(jnp.float32)
    offs = jnp.dot(stri, totals, precision=lax.Precision.HIGHEST)
    cum = (within + offs[:, None, :]).reshape(count, devices)
    return jnp.sum(cum * onehot, axis=1).astype(jnp.int32) - 1


def body(
    temp_start,
    heat_input,
    lateral,
    vertical,
    weighting,
    modulus,
    warp_prev,
    joint_cell,
    joint_owner,
    joint_strain,
    joint_resist,
):
    devices = lax.axis_size(FLAT)
    n_gx, n_gy = (lax.axis_size("gx"), lax.axis_size("gy"))
    gi, gj = (lax.axis_index("gx"), lax.axis_index("gy"))
    rm, cm = warp_prev.shape
    wm = with_halo(jnp.stack([warp_prev, modulus]), (("gx", 1), ("gy", 2)), SWEEPS)
    owners = joint_owner[:, 0]
    capacity = joint_resist.shape[1] // devices
    slots = owners * capacity + joint_ranks(owners, devices)
    temp = thermal(temp_start, heat_input, lateral, vertical)
    load_t = moment_of(temp, weighting)
    load, top = relay(load_t, temp[-1], SWEEPS - 1)
    warp = wm[0]
    mod_ext = wm[1]
    for step in range(1, SWEEPS + 1):
        r = SWEEPS - step
        off = SWEEPS - (r + 1)
        e_pad = mod_ext[off : off + rm + 2 * r + 2, off : off + cm + 2 * r + 2]
        lo = SWEEPS - 1 - r
        ld = load[lo : lo + rm + 2 * r, lo : lo + cm + 2 * r]
        warp = sweep(warp, e_pad, ld)
        if r > 0:
            gr = gi * rm + jnp.arange(-r, rm + r)
            gc = gj * cm + jnp.arange(-r, cm + r)
            inside = ((gr >= 0) & (gr < n_gx * rm))[:, None] & ((gc >= 0) & (gc < n_gy * cm))[
                None, :
            ]
            warp = jnp.where(inside, warp, 0.0)
    fields = jnp.stack([(warp - warp_prev).reshape(-1), top.reshape(-1)])
    picked = fields[:, joint_cell]
    values = jnp.concatenate([picked, jnp.ones_like(picked[:1])], axis=0)
    outgoing = jnp.zeros((3, devices * capacity), jnp.float32).at[:, slots].set(values)
    incoming = lax.all_to_all(outgoing, FLAT, split_axis=1, concat_axis=1, tiled=True)
    strain_next, resist_next = anand(joint_strain, joint_resist, incoming[:, None, :])
    return (warp, strain_next, resist_next)


def solution(mesh):
    return jax.shard_map(
        body,
        mesh=mesh,
        in_specs=(
            P(None, FLAT, None),
            P(None, FLAT, None),
            P(),
            P(),
            P(),
            P("gx", "gy"),
            P("gx", "gy"),
            P(FLAT),
            P(FLAT, None),
            P(None, FLAT, None),
            P(FLAT, None),
        ),
        out_specs=(P("gx", "gy"), P(None, FLAT, None), P(FLAT, None)),
        check_vma=False,
    )
```

profile of v0, /device:TPU:0, one launch (start us, length us, event | category | flops | bytes accessed | tf_op | source)
XLA Modules:
  0.0 136.8 jit_solution(4110263155972718763)
XLA Ops:
  0.7 1.4 %fusion.88 = (f32[8,2,2048]{2,1,0:T(2,128)S(1)}, f32[8,2,2048]{2,1,0:T(2,128)S(1)}) fusion(f32[8,32,2048]{2,1,0:T(8,128)} %param.11), kind=kLoop, calls=%fused_computation.191 | loop fusion | bytes 524288 | tf_op jit(solution)/shard_map/slice | solution.py:89
  2.1 1.3 fusion.89
  3.5 5.0 %collective-permute-start = (f32[8,3,2048]{2,1,0:T(4,128)S(1)}, f32[8,3,2048]{2,1,0:T(4,128)S(1)}, u32[]{:S(2)}, u32[]{:S(2)}) collective-permute-start(f32[8,3,2048]{2,1,0:T(4,128)S(1)} %pad_maximum_fusion.5), channel_id=1, source_target_pairs={{0,1},{1,2},{2,3},{3,4},{4,5},{5,6},{6,7},{7,8},{8,9},{9,10},{10,1... | collective-permute-start | bytes 589832 | tf_op jit(solution)/shard_map/ppermute | solution.py:21
  8.6 1.3 collective-permute-start.1
  9.9 0.8 pad_maximum_fusion.14
  10.7 4.7 %collective-permute-start.4 = (f32[2,3,512]{2,1,0:T(4,128)S(1)}, f32[2,3,512]{2,1,0:T(4,128)S(1)}, u32[]{:S(2)}, u32[]{:S(2)}) collective-permute-start(f32[2,3,512]{2,1,0:T(4,128)S(1)} %get-tuple-element.31), channel_id=1, source_target_pairs={{0,4},{4,8},{8,12},{12,16},{16,20},{20,24},{24,28},{1,5},{5,9},{9,... | collective-permute-start | bytes 36872 | tf_op jit(solution)/shard_map/ppermute | solution.py:21
  15.4 1.3 collective-permute-start.5
  16.7 1.6 %fusion.94 = (f32[1]{0:T(128)}, f32[1]{0:T(128)}, f32[1]{0:T(128)}, f32[1]{0:T(128)}, f32[1]{0:T(128)}, /*index=5*/f32[1]{0:T(128)}, f32[1]{0:T(128)}, f32[1]{0:T(128)}) fusion(f32[8]{0:T(128)} %param.15), kind=kLoop, calls=%fused_computation.197 | loop fusion | bytes 64 | tf_op jit(solution)/shard_map/slice | solution.py:44
  18.3 0.9 convolution_bitcast_fusion
  19.9 3.4 %collective-permute-done.1 = f32[8,3,2048]{2,1,0:T(4,128)S(1)} collective-permute-done((f32[8,3,2048]{2,1,0:T(4,128)S(1)}, f32[8,3,2048]{2,1,0:T(4,128)S(1)}, u32[]{:S(2)}, u32[]{:S(2)}) %collective-permute-start.1) | collective-permute-done | bytes 196640 | tf_op jit(solution)/shard_map/ppermute | solution.py:21
  24.3 1.0 copy-done.1
  25.3 3.0 %fusion.7 = f32[8,34,2048]{2,1,0:T(8,128)S(1)} fusion(f32[8,36,2048]{2,1,0:T(8,128)S(1)} %pad_maximum_fusion, f32[8,2,2048]{2,1,0:T(2,128)S(1)} %slice.403, f32[8,32,2048]{2,1,0:T(8,128)S(1)} %copy-done, f32[8,2,2048]{2,1,0:T(2,128)S(1)} %slice.402, f32[8,1,2048]{2,1,0:T(1,128)S(1)} %slice.408, f32[8,32,2048]{2,1,0:T(8,128)S(1)} %copy-done.1, ...), kind=kLoop, calls=%fused_computation.13 | loop fusion | flops 8355840 | bytes 14353408 | tf_op jit(solution)/shard_map/jit(_where)/select_n | solution.py:101
  28.8 1.9 %fusion.15 = f32[8,32,2048]{2,1,0:T(8,128)S(1)} fusion(f32[8,32,2048]{2,1,0:T(8,128)S(1)} %copy-done.1, f32[8,34,2048]{2,1,0:T(8,128)S(1)} %fusion.7, f32[7,32,2048]{2,1,0:T(8,128)S(1)} %fusion.16, f32[8]{0:T(128)S(1)} %copy-done.9), kind=kLoop, calls=%fused_computation.24 | loop fusion | flops 5242880 | bytes 14942720 | tf_op jit(solution)/shard_map/add | solution.py:40
  30.7 5.2 %fusion.54 = f32[32,2048]{1,0:T(8,128)S(1)} fusion(f32[8,32,2048]{2,1,0:T(8,128)S(1)} %fusion.15, f32[]{:T(128)} %bitcast.8, f32[]{:T(128)} %bitcast.6, f32[]{:T(128)} %bitcast.5, f32[]{:T(128)} %bitcast.4, f32[]{:T(128)} %bitcast.3, f32[]{:T(128)} %bitcast.2, f32[]{:T(128)} %bitcast.1, f32[]{:T(128)} %bitcast), kind=kLoop, calls=%fused_computation.109 | loop fusion | flops 983040 | bytes 2359328 | tf_op jit(solution)/shard_map/add | solution.py:46
  35.9 2.5 %collective-permute-start.2 = (f32[2,2048]{1,0:T(2,128)S(1)}, f32[2,2048]{1,0:T(2,128)S(1)}, u32[]{:S(2)}, u32[]{:S(2)}) collective-permute-start(f32[2,2048]{1,0:T(2,128)S(1)} %get-tuple-element.33), channel_id=1, source_target_pairs={{0,1},{1,2},{2,3},{3,4},{4,5},{5,6},{6,7},{7,8},{8,9},{9,10},{10,1... | collective-permute-start | bytes 49160 | tf_op jit(solution)/shard_map/ppermute | solution.py:21
  38.4 1.3 collective-permute-start.3
  40.1 3.9 %collective-permute-done.3 = f32[2,2048]{1,0:T(2,128)S(1)} collective-permute-done((f32[2,2048]{1,0:T(2,128)S(1)}, f32[2,2048]{1,0:T(2,128)S(1)}, u32[]{:S(2)}, u32[]{:S(2)}) %collective-permute-start.3) | collective-permute-done | bytes 16416 | tf_op jit(solution)/shard_map/ppermute | solution.py:21
  45.3 1.2 pad_maximum_fusion.1
  46.5 5.4 %all-to-all-start = ((f32[4,2,36,516]{3,1,2,0:T(2,128)}), f32[4,2,36,516]{3,1,2,0:T(2,128)S(1)}, u32[]{:S(2)}, u32[]{:S(2)}) async-start(f32[4,2,36,516]{3,1,2,0:T(2,128)} %pad_maximum_fusion.1), calls=%async_computation | async-start | bytes 1474560 | tf_op jit(solution)/shard_map/all_to_all | solution.py:115
  52.1 3.9 %collective-permute-start.6 = (f32[2,134,3]{2,1,0:T(8,128)S(1)}, f32[2,134,3]{2,1,0:T(8,128)S(1)}, u32[]{:S(2)}, u32[]{:S(2)}) collective-permute-start(f32[2,134,3]{2,1,0:T(8,128)S(1)} %get-tuple-element.29), channel_id=1, source_target_pairs={{0,1},{1,2},{2,3},{4,5},{5,6},{6,7},{8,9},{9,10},{10,11},{12,13},{... | collective-permute-start | bytes 9656 | tf_op jit(solution)/shard_map/ppermute | solution.py:21
  56.0 1.5 %collective-permute-start.7 = (f32[2,134,3]{2,1,0:T(8,128)S(1)}, f32[2,134,3]{2,1,0:T(8,128)S(1)}, u32[]{:S(2)}, u32[]{:S(2)}) collective-permute-start(f32[2,134,3]{2,1,0:T(8,128)S(1)} %get-tuple-element.30), channel_id=1, source_target_pairs={{1,0},{2,1},{3,2},{5,4},{6,5},{7,6},{9,8},{10,9},{11,10},{13,12},{... | collective-permute-start | bytes 9656 | tf_op jit(solution)/shard_map/ppermute | solution.py:21
  57.5 9.2 %collective-permute-done.6 = f32[2,134,3]{2,1,0:T(8,128)S(1)} collective-permute-done((f32[2,134,3]{2,1,0:T(8,128)S(1)}, f32[2,134,3]{2,1,0:T(8,128)S(1)}, u32[]{:S(2)}, u32[]{:S(2)}) %collective-permute-start.6) | collective-permute-done | bytes 3248 | tf_op jit(solution)/shard_map/ppermute | solution.py:21
  67.1 4.3 %all-to-all-done = f32[4,2,36,516]{3,1,2,0:T(2,128)S(1)} async-done(((f32[4,2,36,516]{3,1,2,0:T(2,128)}), f32[4,2,36,516]{3,1,2,0:T(2,128)S(1)}, u32[]{:S(2)}, u32[]{:S(2)}) %all-to-all-start) | async-done | bytes 594464 | tf_op jit(solution)/shard_map/all_to_all | solution.py:115
  71.3 0.8 fusion.90
  73.5 0.9 fusion.23
  74.4 1.4 %subtract_bitcast_fusion = (f32[1,1,128,512]{3,2,1,0:T(8,128)S(1)}, f32[128,512]{1,0:T(8,128)}) fusion(f32[128,512]{1,0:T(8,128)S(1)} %copy-done.2, f32[130,514]{1,0:T(8,128)S(1)} %fusion.23, f32[134,518]{1,0:T(8,128)S(1)} %get-tuple-element.23, f32[132,516]{1,0:T(8,128)S(1)} %get-tuple-element.10), kind=kLoop, calls=%fused_computation.124 | loop fusion | flops 1441792 | bytes 3407872
  76.6 15.6 %copy.24 = f32[2,65536]{0,1:T(8,128)} copy(f32[2,65536]{1,0:T(2,128)S(1)} %pad_maximum_fusion.3) | data formatting | bytes 1048576 | tf_op jit(solution)/shard_map/stack | solution.py:185
  92.2 18.2 %gather_fusion = f32[2048,2]{1,0:T(8,128)} fusion(f32[2,65536]{0,1:T(8,128)} %copy.24, s32[2048]{0:T(1024)S(1)} %fusion.79), kind=kCustom, calls=%fused_computation | custom fusion | bytes 40960 | tf_op jit(solution)/shard_map/gather | solution.py:186
  110.4 6.8 %scatter_custom_fusion = f32[3,6144]{0,1:T(8,128)S(1)} fusion(s32[2048]{0:T(1024)S(1)} %bitcast.102, f32[]{:T(128)} %constant.34.clone.1, f32[2,2048]{0,1:T(8,128)} %bitcast.96, f32[]{:T(128)} %constant.45.clone.1), kind=kCustom, calls=%fused_computation.28 | custom fusion | bytes 90120 | tf_op jit(solution)/shard_map/scatter | solution.py:188
  117.2 1.5 %copy.25 = f32[3,32,192]{2,0,1:T(4,128)S(1)} copy(f32[3,32,192]{0,2,1:T(8,128)S(1)} %bitcast.89) | data formatting | bytes 147456 | tf_op jit(solution)/shard_map/all_to_all | solution.py:189
  118.7 15.4 %all_to_all.14 = f32[3,32,192]{2,0,1:T(4,128)S(1)} all-to-all(f32[3,32,192]{2,0,1:T(4,128)S(1)} %copy.25), channel_id=1, replica_groups=mesh['gx'=8,'gy'=4] {'gx','gy'}, dimensions={1} | all-to-all | bytes 147456 | tf_op jit(solution)/shard_map/all_to_all | solution.py:189
  134.9 1.1 add_select_fusion
  (75 shorter events, 8.0 us)
Async XLA Ops:
  0.6 22.7 %copy-start = (f32[8,32,2048]{2,1,0:T(8,128)S(1)}, f32[8,32,2048]{2,1,0:T(8,128)}, u32[]{:S(2)}) copy-start(f32[8,32,2048]{2,1,0:T(8,128)} %param.11) | copy-start | bytes 6291460
  0.6 19.0 %copy-start.5 = (s32[2048,1]{0,1:T(1,128)S(1)}, s32[2048,1]{0,1:T(1,128)}, u32[]{:S(2)}) copy-start(s32[2048,1]{0,1:T(1,128)} %param.19) | copy-start | bytes 24580
  0.7 19.2 %copy-start.7 = (s32[2048]{0:T(1024)S(1)}, s32[2048]{0:T(1024)}, u32[]{:S(2)}) copy-start(s32[2048]{0:T(1024)} %param.18) | copy-start | bytes 24580
  3.5 16.3 %collective-permute-start = (f32[8,3,2048]{2,1,0:T(4,128)S(1)}, f32[8,3,2048]{2,1,0:T(4,128)S(1)}, u32[]{:S(2)}, u32[]{:S(2)}) collective-permute-start(f32[8,3,2048]{2,1,0:T(4,128)S(1)} %pad_maximum_fusion.5), channel_id=1, source_target_pairs={{0,1},{1,2},{2,3},{3,4},{4,5},{5,6},{6,7},{7,8},{8,9},{9,10},{10,1... | collective-permute-start | bytes 589832 | tf_op jit(solution)/shard_map/ppermute | solution.py:21
  8.6 14.6 %collective-permute-start.1 = (f32[8,3,2048]{2,1,0:T(4,128)S(1)}, f32[8,3,2048]{2,1,0:T(4,128)S(1)}, u32[]{:S(2)}, u32[]{:S(2)}) collective-permute-start(f32[8,3,2048]{2,1,0:T(4,128)S(1)} %pad_maximum_fusion.6), channel_id=1, source_target_pairs={{1,0},{2,1},{3,2},{4,3},{5,4},{6,5},{7,6},{8,7},{9,8},{10,9},{11,1... | collective-permute-start | bytes 589832 | tf_op jit(solution)/shard_map/ppermute | solution.py:21
  10.7 41.2 %collective-permute-start.4 = (f32[2,3,512]{2,1,0:T(4,128)S(1)}, f32[2,3,512]{2,1,0:T(4,128)S(1)}, u32[]{:S(2)}, u32[]{:S(2)}) collective-permute-start(f32[2,3,512]{2,1,0:T(4,128)S(1)} %get-tuple-element.31), channel_id=1, source_target_pairs={{0,4},{4,8},{8,12},{12,16},{16,20},{20,24},{24,28},{1,5},{5,9},{9,... | collective-permute-start | bytes 36872 | tf_op jit(solution)/shard_map/ppermute | solution.py:21
  15.4 36.5 %collective-permute-start.5 = (f32[2,3,512]{2,1,0:T(4,128)S(1)}, f32[2,3,512]{2,1,0:T(4,128)S(1)}, u32[]{:S(2)}, u32[]{:S(2)}) collective-permute-start(f32[2,3,512]{2,1,0:T(4,128)S(1)} %get-tuple-element.32), channel_id=1, source_target_pairs={{4,0},{8,4},{12,8},{16,12},{20,16},{24,20},{28,24},{5,1},{9,5},{13... | collective-permute-start | bytes 36872 | tf_op jit(solution)/shard_map/ppermute | solution.py:21
  19.9 3.8 %copy-start.8 = (f32[7]{0:T(128)S(1)}, f32[7]{0:T(128)}, u32[]{:S(2)}) copy-start(f32[7]{0:T(128)} %param.14) | copy-start | bytes 88
  23.7 1.6 %copy-start.1 = (f32[8,32,2048]{2,1,0:T(8,128)S(1)}, f32[8,32,2048]{2,1,0:T(8,128)}, u32[]{:S(2)}) copy-start(f32[8,32,2048]{2,1,0:T(8,128)} %param.12) | copy-start | bytes 6291460
  23.8 1.6 %copy-start.9 = (f32[8]{0:T(128)S(1)}, f32[8]{0:T(128)}, u32[]{:S(2)}) copy-start(f32[8]{0:T(128)} %param.13) | copy-start | bytes 100
  35.9 4.2 %collective-permute-start.2 = (f32[2,2048]{1,0:T(2,128)S(1)}, f32[2,2048]{1,0:T(2,128)S(1)}, u32[]{:S(2)}, u32[]{:S(2)}) collective-permute-start(f32[2,2048]{1,0:T(2,128)S(1)} %get-tuple-element.33), channel_id=1, source_target_pairs={{0,1},{1,2},{2,3},{3,4},{4,5},{5,6},{6,7},{7,8},{8,9},{9,10},{10,1... | collective-permute-start | bytes 49160 | tf_op jit(solution)/shard_map/ppermute | solution.py:21
  38.4 5.6 %collective-permute-start.3 = (f32[2,2048]{1,0:T(2,128)S(1)}, f32[2,2048]{1,0:T(2,128)S(1)}, u32[]{:S(2)}, u32[]{:S(2)}) collective-permute-start(f32[2,2048]{1,0:T(2,128)S(1)} %get-tuple-element.34), channel_id=1, source_target_pairs={{1,0},{2,1},{3,2},{4,3},{5,4},{6,5},{7,6},{8,7},{9,8},{10,9},{11,1... | collective-permute-start | bytes 49160 | tf_op jit(solution)/shard_map/ppermute | solution.py:21
  44.2 7.7 %copy-start.2 = (f32[128,512]{1,0:T(8,128)S(1)}, f32[128,512]{1,0:T(8,128)}, u32[]{:S(2)}) copy-start(f32[128,512]{1,0:T(8,128)} %param.17) | copy-start | bytes 786436
  44.2 7.7 %copy-start.3 = (f32[128,512]{1,0:T(8,128)S(1)}, f32[128,512]{1,0:T(8,128)}, u32[]{:S(2)}) copy-start(f32[128,512]{1,0:T(8,128)} %param.16) | copy-start | bytes 786436
  46.5 24.8 %all-to-all-start = ((f32[4,2,36,516]{3,1,2,0:T(2,128)}), f32[4,2,36,516]{3,1,2,0:T(2,128)S(1)}, u32[]{:S(2)}, u32[]{:S(2)}) async-start(f32[4,2,36,516]{3,1,2,0:T(2,128)} %pad_maximum_fusion.1), calls=%async_computation | async-start | bytes 1474560 | tf_op jit(solution)/shard_map/all_to_all | solution.py:115
  52.1 14.6 %collective-permute-start.6 = (f32[2,134,3]{2,1,0:T(8,128)S(1)}, f32[2,134,3]{2,1,0:T(8,128)S(1)}, u32[]{:S(2)}, u32[]{:S(2)}) collective-permute-start(f32[2,134,3]{2,1,0:T(8,128)S(1)} %get-tuple-element.29), channel_id=1, source_target_pairs={{0,1},{1,2},{2,3},{4,5},{5,6},{6,7},{8,9},{9,10},{10,11},{12,13},{... | collective-permute-start | bytes 9656 | tf_op jit(solution)/shard_map/ppermute | solution.py:21
  56.0 10.7 %collective-permute-start.7 = (f32[2,134,3]{2,1,0:T(8,128)S(1)}, f32[2,134,3]{2,1,0:T(8,128)S(1)}, u32[]{:S(2)}, u32[]{:S(2)}) collective-permute-start(f32[2,134,3]{2,1,0:T(8,128)S(1)} %get-tuple-element.30), channel_id=1, source_target_pairs={{1,0},{2,1},{3,2},{5,4},{6,5},{7,6},{9,8},{10,9},{11,10},{13,12},{... | collective-permute-start | bytes 9656 | tf_op jit(solution)/shard_map/ppermute | solution.py:21
  117.2 17.7 %copy-start.4 = (f32[2,1,6144]{2,1,0:T(1,128)S(1)}, f32[2,1,6144]{2,1,0:T(1,128)}, u32[]{:S(2)}) copy-start(f32[2,1,6144]{2,1,0:T(1,128)} %param.20) | copy-start | bytes 147460
  117.2 17.7 %copy-start.6 = (f32[1,6144]{1,0:T(1,128)S(1)}, f32[1,6144]{1,0:T(1,128)}, u32[]{:S(2)}) copy-start(f32[1,6144]{1,0:T(1,128)} %param.21) | copy-start | bytes 73732
where the time goes:
time: 137 us
  local copies, waits for them, and re-layouts  51 us (37%)
  starting transfers between devices  26.7 us (19%)
  waiting for transfers between devices  20.8 us (15%)
  other arithmetic  20.7 us (15%)
  blocking collectives  15.4 us (11%)
    ppermute x8, starting transfers between devices, exchange(): return (lax.ppermute(last, axis, up), lax.ppermute(leading, axis, down))  21.4 us
    gather x1, local copies, waits for them, and re-layouts, body(): picked = fields[:, joint_cell]  18.2 us
    ppermute x8, waiting for transfers between devices, exchange(): return (lax.ppermute(last, axis, up), lax.ppermute(leading, axis, down))  16.5 us
    another operation x1, local copies, waits for them, and re-layouts, body(): fields = jnp.stack([(warp - warp_prev).reshape(-1), top.reshape(-1)])  15.6 us
    all_to_all x1, blocking collectives, body(): lax.all_to_all(outgoing, FLAT, split_axis=1, concat_axis=1, tiled=True)  15.4 us
    scatter x1, local copies, waits for them, and re-layouts, body(): jnp.zeros((3, devices * capacity), jnp.float32).at[:, slots].set(values)  6.81 us
    all_to_all x1, starting transfers between devices, relay(): recv = lax.all_to_all(send, 'gy', split_axis=0, concat_axis=0, tiled=True)  5.38 us
    add x1, other arithmetic, moment_of(): total = total + weighting[layer] * field[layer]  5.21 us
  transfers between devices with their start and end apart: 9, of which 4 were waited for; matrix products, arithmetic and copies ran while one was open for 14% of the time, Pallas kernels for 0%

commit v1 on v0

--- a/solution.py
+++ b/solution.py
@@ -12,6 +12,22 @@
 sat_power = 0.3
 harden = 2.0
 FLAT = ("gx", "gy")
+
+
+def spread_slot_by_axis(unit, in_dim, local):
+    v_next, current_value = (unit.shape[:in_dim], unit.shape[in_dim + 1 :])
+    block_last = unit.reshape(*v_next, local, -1, *current_value)
+    a_now = jnp.moveaxis(block_last, in_dim, 0)
+    return a_now
+
+
+def move_trails_over_axis(u, array_axis):
+    u = jnp.moveaxis(u, 0, array_axis)
+    oldest = u.shape
+    arr_next = u.reshape(
+        *oldest[:array_axis], oldest[array_axis] * oldest[array_axis + 1], *oldest[array_axis + 2 :]
+    )
+    return arr_next
 
 
 def exchange(last, leading, axis):
@@ -103,6 +119,24 @@
 
 
 def relay(load, top, width):
+
+    def spots_deliver(u_in, chip_axis, original, patch):
+        then = lax.axis_size(chip_axis)
+        seen_now = lax.axis_index(chip_axis)
+        latest, d_next = (then, seen_now)
+        carry_out = spread_slot_by_axis(u_in, original, latest)
+        so_far_all = [carry_out[d_next]]
+        for b in range(1, latest):
+            e_now = carry_out[d_next ^ b]
+            x_next = lax.ppermute(
+                e_now, axis_name=chip_axis, perm=[(no, no ^ b) for no in range(latest)]
+            )
+            so_far_all.append(x_next)
+        f_next = jnp.stack(so_far_all, axis=0)
+        carry_out = f_next[d_next ^ jnp.arange(latest)]
+        t1 = move_trails_over_axis(carry_out, patch)
+        return t1
+
     n_gy = lax.axis_size("gy")
     rows, cols = load.shape
     cm = cols // n_gy
@@ -112,7 +146,7 @@
     tp = jnp.pad(top, ((width, width), (width, width)))
     both = jnp.stack([lp, tp])
     send = jnp.stack([both[:, :, k * cm : k * cm + cm + 2 * width] for k in range(n_gy)])
-    recv = lax.all_to_all(send, "gy", split_axis=0, concat_axis=0, tiled=True)
+    recv = spots_deliver(send, "gy", 0, 0)
     parts = []
     for k in range(n_gy):
         lo = 0 if k == 0 else width

time: 137 us -> 144 us (1.051)
  blocking collectives: 15.4 us -> 22.8 us
  waiting for transfers between devices: 20.8 us -> 15.8 us
  other arithmetic: 20.7 us -> 24.6 us
  starting transfers between devices: 26.7 us -> 29.2 us
    ppermute x8, waiting for transfers between devices: 16.5 us -> 5.66 us  [exchange(): return (lax.ppermute(last, axis, up), lax.ppermute(leading, axis, down))]
    ppermute x0 -> x3, waiting for transfers between devices: none -> 10.2 us  [spots_deliver(): lax.ppermute(e_now, axis_name=chip_axis, perm=[(no, no ^ b) for no in ran...]
    all_to_all x1, blocking collectives: 15.4 us -> 22.8 us  [body(): lax.all_to_all(outgoing, FLAT, split_axis=1, concat_axis=1, tiled=True)]
    all_to_all x1 -> x0, starting transfers between devices: 5.38 us -> none  [relay(): recv = lax.all_to_all(send, 'gy', split_axis=0, concat_axis=0, tiled=True)]
    ppermute x0 -> x3, starting transfers between devices: none -> 4.65 us  [spots_deliver(): lax.ppermute(e_now, axis_name=chip_axis, perm=[(no, no ^ b) for no in ran...]
    all_to_all x1 -> x0, waiting for transfers between devices: 4.28 us -> none  [relay(): recv = lax.all_to_all(send, 'gy', split_axis=0, concat_axis=0, tiled=True)]
    ppermute x8, starting transfers between devices: 21.4 us -> 24.5 us  [exchange(): return (lax.ppermute(last, axis, up), lax.ppermute(leading, axis, down))]
    another operation x2, other arithmetic: 1.89 us -> 0.13 us  [relay(): jnp.stack([both[:, :, k * cm:k * cm + cm + 2 * width] for k in range(n_gy)])]
  transfers between devices with their start and end apart: 9 -> 11, of which waited for: 4 -> 6; matrix products, arithmetic and copies ran while one was open for 14% -> 6% of each run, Pallas kernels for 0% -> 0%
where the time goes in v1:
time: 144 us
  local copies, waits for them, and re-layouts  49.9 us (35%)
  starting transfers between devices  29.2 us (20%)
  other arithmetic  24.6 us (17%)
  blocking collectives  22.8 us (16%)
  waiting for transfers between devices  15.8 us (11%)
    ppermute x8, starting transfers between devices, exchange(): return (lax.ppermute(last, axis, up), lax.ppermute(leading, axis, down))  24.5 us
    all_to_all x1, blocking collectives, body(): lax.all_to_all(outgoing, FLAT, split_axis=1, concat_axis=1, tiled=True)  22.8 us
    gather x1, local copies, waits for them, and re-layouts, body(): picked = fields[:, joint_cell]  18.1 us
    another operation x1, local copies, waits for them, and re-layouts, body(): fields = jnp.stack([(warp - warp_prev).reshape(-1), top.reshape(-1)])  15.6 us
    ppermute x3, waiting for transfers between devices, spots_deliver(): lax.ppermute(e_now, axis_name=chip_axis, perm=[(no, no ^ b) for no in ran...  10.2 us
    scatter x1, local copies, waits for them, and re-layouts, body(): jnp.zeros((3, devices * capacity), jnp.float32).at[:, slots].set(values)  6.8 us
    ppermute x8, waiting for transfers between devices, exchange(): return (lax.ppermute(last, axis, up), lax.ppermute(leading, axis, down))  5.66 us
    add x1, other arithmetic, moment_of(): total = total + weighting[layer] * field[layer]  5.15 us
  transfers between devices with their start and end apart: 11, of which 6 were waited for; matrix products, arithmetic and copies ran while one was open for 6% of the time, Pallas kernels for 0%

profile of v1, /device:TPU:0, one launch (start us, length us, event | category | flops | bytes accessed | tf_op | source)
XLA Modules:
  0.0 143.8 jit_solution(8150656457417252597)
XLA Ops:
  0.7 1.4 fusion.89
  2.1 1.3 fusion.90
  3.5 5.0 %collective-permute-start = (f32[8,3,2048]{2,0,1:T(8,128)S(1)}, f32[8,3,2048]{2,0,1:T(8,128)S(1)}, u32[]{:S(2)}, u32[]{:S(2)}) collective-permute-start(f32[8,3,2048]{2,0,1:T(8,128)S(1)} %pad_maximum_fusion.6), channel_id=1, source_target_pairs={{0,1},{1,2},{2,3},{3,4},{4,5},{5,6},{6,7},{7,8},{8,9},{9,10},{10,1... | collective-permute-start | bytes 589832 | tf_op jit(solution)/shard_map/ppermute | solution.py:37
  8.6 1.3 collective-permute-start.1
  9.9 0.9 pad_maximum_fusion.14
  10.9 4.7 %collective-permute-start.7 = (f32[2,3,512]{2,1,0:T(4,128)S(1)}, f32[2,3,512]{2,1,0:T(4,128)S(1)}, u32[]{:S(2)}, u32[]{:S(2)}) collective-permute-start(f32[2,3,512]{2,1,0:T(4,128)S(1)} %get-tuple-element.35), channel_id=1, source_target_pairs={{0,4},{4,8},{8,12},{12,16},{16,20},{20,24},{24,28},{1,5},{5,9},{9,... | collective-permute-start | bytes 36872 | tf_op jit(solution)/shard_map/ppermute | solution.py:37
  15.5 1.3 collective-permute-start.8
  21.8 0.8 pad_maximum_fusion.11
  22.6 1.3 collective-permute-start.10
  23.9 5.2 %collective-permute-start.9 = (f32[2,134,3]{2,1,0:T(8,128)}, f32[2,134,3]{2,1,0:T(8,128)}, u32[]{:S(2)}, u32[]{:S(2)}) collective-permute-start(f32[2,134,3]{2,1,0:T(8,128)} %get-tuple-element.33), channel_id=1, source_target_pairs={{0,1},{1,2},{2,3},{4,5},{5,6},{6,7},{8,9},{9,10},{10,11},{12,13},{... | collective-permute-start | bytes 9656 | tf_op jit(solution)/shard_map/ppermute | solution.py:37
  29.8 1.6 %collective-permute-done.9 = f32[2,134,3]{2,1,0:T(8,128)} collective-permute-done((f32[2,134,3]{2,1,0:T(8,128)}, f32[2,134,3]{2,1,0:T(8,128)}, u32[]{:S(2)}, u32[]{:S(2)}) %collective-permute-start.9) | collective-permute-done | bytes 3248 | tf_op jit(solution)/shard_map/ppermute | solution.py:37
  31.4 1.2 pad_maximum_fusion.2
  34.1 1.1 copy-done.1
  35.2 3.0 %fusion.7 = f32[8,34,2048]{2,1,0:T(8,128)S(1)} fusion(f32[8,36,2048]{2,1,0:T(8,128)S(1)} %pad_maximum_fusion, f32[8,2,2048]{2,1,0:T(2,128)S(1)} %copy.22, f32[8,32,2048]{2,1,0:T(8,128)S(1)} %copy-done, f32[8,2,2048]{2,1,0:T(2,128)S(1)} %copy.21, f32[8,1,2048]{2,1,0:T(1,128)S(1)} %copy.26, f32[8,32,2048]{2,1,0:T(8,128)S(1)} %copy-done.1, ...), kind=kLoop, calls=%fused_computation.14 | loop fusion | flops 8355840 | bytes 14353408 | tf_op jit(solution)/shard_map/jit(_where)/select_n | solution.py:117
  38.6 2.0 %fusion.15 = f32[8,32,2048]{2,1,0:T(8,128)S(1)} fusion(f32[8,32,2048]{2,1,0:T(8,128)S(1)} %copy-done.1, f32[8,34,2048]{2,1,0:T(8,128)S(1)} %fusion.7, f32[7,32,2048]{2,1,0:T(8,128)S(1)} %fusion.16, f32[8]{0:T(128)S(1)} %copy-done.12), kind=kLoop, calls=%fused_computation.25 | loop fusion | flops 5242880 | bytes 14942720 | tf_op jit(solution)/shard_map/add | solution.py:56
  40.7 5.2 %fusion.54 = f32[32,2048]{1,0:T(8,128)S(1)} fusion(f32[8,32,2048]{2,1,0:T(8,128)S(1)} %fusion.15, f32[]{:T(128)} %bitcast.8, f32[]{:T(128)} %bitcast.6, f32[]{:T(128)} %bitcast.5, f32[]{:T(128)} %bitcast.4, f32[]{:T(128)} %bitcast.3, f32[]{:T(128)} %bitcast.2, f32[]{:T(128)} %bitcast.1, f32[]{:T(128)} %bitcast), kind=kLoop, calls=%fused_computation.112 | loop fusion | flops 983040 | bytes 2359328 | tf_op jit(solution)/shard_map/add | solution.py:62
  45.9 4.4 %collective-permute-start.2 = (f32[2,2048]{1,0:T(2,128)S(1)}, f32[2,2048]{1,0:T(2,128)S(1)}, u32[]{:S(2)}, u32[]{:S(2)}) collective-permute-start(f32[2,2048]{1,0:T(2,128)S(1)} %get-tuple-element.37), channel_id=1, source_target_pairs={{0,1},{1,2},{2,3},{3,4},{4,5},{5,6},{6,7},{7,8},{8,9},{9,10},{10,1... | collective-permute-start | bytes 49160 | tf_op jit(solution)/shard_map/ppermute | solution.py:37
  50.2 1.5 %collective-permute-start.3 = (f32[2,2048]{1,0:T(2,128)S(1)}, f32[2,2048]{1,0:T(2,128)S(1)}, u32[]{:S(2)}, u32[]{:S(2)}) collective-permute-start(f32[2,2048]{1,0:T(2,128)S(1)} %get-tuple-element.38), channel_id=1, source_target_pairs={{1,0},{2,1},{3,2},{4,3},{5,4},{6,5},{7,6},{8,7},{9,8},{10,9},{11,1... | collective-permute-start | bytes 49160 | tf_op jit(solution)/shard_map/ppermute | solution.py:37
  51.9 4.0 %collective-permute-done.3 = f32[2,2048]{1,0:T(2,128)S(1)} collective-permute-done((f32[2,2048]{1,0:T(2,128)S(1)}, f32[2,2048]{1,0:T(2,128)S(1)}, u32[]{:S(2)}, u32[]{:S(2)}) %collective-permute-start.3) | collective-permute-done | bytes 16416 | tf_op jit(solution)/shard_map/ppermute | solution.py:37
  56.4 4.6 %collective-permute-start.5 = (f32[1,2,36,516]{3,2,1,0:T(8,128)S(1)}, f32[1,2,36,516]{3,2,1,0:T(8,128)S(1)}, u32[]{:S(2)}, u32[]{:S(2)}) collective-permute-start(f32[1,2,36,516]{3,2,1,0:T(8,128)S(1)} %get-tuple-element.25), channel_id=1, source_target_pairs={{0,2},{1,3},{2,0},{3,1},{4,6},{5,7},{6,4},{7,5},{8,10},{9,11},{10,... | collective-permute-start | bytes 445832 | tf_op jit(solution)/shard_map/ppermute | solution.py:131
  61.0 4.2 %collective-permute-done.4 = f32[1,2,36,516]{3,2,1,0:T(8,128)S(1)} collective-permute-done((f32[1,2,36,516]{3,2,1,0:T(8,128)S(1)}, f32[1,2,36,516]{3,2,1,0:T(8,128)S(1)}, u32[]{:S(2)}, u32[]{:S(2)}) %collective-permute-start.4) | collective-permute-done | bytes 148640 | tf_op jit(solution)/shard_map/ppermute | solution.py:131
  65.1 2.7 %collective-permute-done.5 = f32[1,2,36,516]{3,2,1,0:T(8,128)S(1)} collective-permute-done((f32[1,2,36,516]{3,2,1,0:T(8,128)S(1)}, f32[1,2,36,516]{3,2,1,0:T(8,128)S(1)}, u32[]{:S(2)}, u32[]{:S(2)}) %collective-permute-start.5) | collective-permute-done | bytes 148640 | tf_op jit(solution)/shard_map/ppermute | solution.py:131
  67.9 3.3 %collective-permute-done.6 = f32[1,2,36,516]{3,2,1,0:T(8,128)S(1)} collective-permute-done((f32[1,2,36,516]{3,2,1,0:T(8,128)S(1)}, f32[1,2,36,516]{3,2,1,0:T(8,128)S(1)}, u32[]{:S(2)}, u32[]{:S(2)}) %collective-permute-start.6) | collective-permute-done | bytes 148640 | tf_op jit(solution)/shard_map/ppermute | solution.py:131
  72.5 0.7 fusion.32
  73.2 0.9 fusion.23
  74.2 1.4 subtract_bitcast_fusion
  76.4 15.6 %copy.27 = f32[2,65536]{0,1:T(8,128)} copy(f32[2,65536]{1,0:T(2,128)S(1)} %pad_maximum_fusion.3) | data formatting | bytes 1048576 | tf_op jit(solution)/shard_map/stack | solution.py:219
  91.9 18.1 %gather_fusion.1 = f32[2048,2]{1,0:T(8,128)} fusion(f32[2,65536]{0,1:T(8,128)} %copy.27, s32[2048]{0:T(1024)S(1)} %fusion.79), kind=kCustom, calls=%fused_computation.1 | custom fusion | bytes 40960 | tf_op jit(solution)/shard_map/gather | solution.py:220
  110.0 6.8 %scatter_custom_fusion = f32[3,6144]{0,1:T(8,128)S(1)} fusion(s32[2048]{0:T(1024)} %bitcast.116, f32[]{:T(128)} %constant.37.clone.1, f32[2,2048]{0,1:T(8,128)} %bitcast.107, f32[]{:T(128)} %constant.51.clone.1), kind=kCustom, calls=%fused_computation.29 | custom fusion | bytes 1123328 | tf_op jit(solution)/shard_map/scatter | solution.py:222
  116.9 1.5 %copy.28 = f32[3,32,192]{2,0,1:T(4,128)S(1)} copy(f32[3,32,192]{0,2,1:T(8,128)S(1)} %bitcast.100) | data formatting | bytes 147456 | tf_op jit(solution)/shard_map/all_to_all | solution.py:223
  118.4 22.8 %all_to_all.9 = f32[3,32,192]{2,0,1:T(4,128)S(1)} all-to-all(f32[3,32,192]{2,0,1:T(4,128)S(1)} %copy.28), channel_id=1, replica_groups=mesh['gx'=8,'gy'=4] {'gx','gy'}, dimensions={1} | all-to-all | bytes 147456 | tf_op jit(solution)/shard_map/all_to_all | solution.py:223
  141.9 1.1 add_select_fusion
  (102 shorter events, 11.9 us)
Async XLA Ops:
  0.6 21.2 %copy-start.2 = (f32[128,512]{1,0:T(8,128)S(1)}, f32[128,512]{1,0:T(8,128)}, u32[]{:S(2)}) copy-start(f32[128,512]{1,0:T(8,128)} %param.17) | copy-start | bytes 786436
  0.6 21.2 %copy-start.3 = (f32[128,512]{1,0:T(8,128)S(1)}, f32[128,512]{1,0:T(8,128)}, u32[]{:S(2)}) copy-start(f32[128,512]{1,0:T(8,128)} %param.16) | copy-start | bytes 786436
  0.7 17.4 %copy-start.8 = (f32[8]{0:T(128)S(1)}, f32[8]{0:T(128)}, u32[]{:S(2)}) copy-start(f32[8]{0:T(128)} %param.15) | copy-start | bytes 100
  0.7 19.1 %copy-start.10 = (s32[2048]{0:T(1024)S(1)}, s32[2048]{0:T(1024)}, u32[]{:S(2)}) copy-start(s32[2048]{0:T(1024)} %param.18) | copy-start | bytes 24580
  0.7 19.1 %copy-start.5 = (s32[2048,1]{0,1:T(1,128)S(1)}, s32[2048,1]{0,1:T(1,128)}, u32[]{:S(2)}) copy-start(s32[2048,1]{0,1:T(1,128)} %param.19) | copy-start | bytes 24580
  3.5 29.1 %collective-permute-start = (f32[8,3,2048]{2,0,1:T(8,128)S(1)}, f32[8,3,2048]{2,0,1:T(8,128)S(1)}, u32[]{:S(2)}, u32[]{:S(2)}) collective-permute-start(f32[8,3,2048]{2,0,1:T(8,128)S(1)} %pad_maximum_fusion.6), channel_id=1, source_target_pairs={{0,1},{1,2},{2,3},{3,4},{4,5},{5,6},{6,7},{7,8},{8,9},{9,10},{10,1... | collective-permute-start | bytes 589832 | tf_op jit(solution)/shard_map/ppermute | solution.py:37
  8.6 24.1 %collective-permute-start.1 = (f32[8,3,2048]{2,0,1:T(8,128)S(1)}, f32[8,3,2048]{2,0,1:T(8,128)S(1)}, u32[]{:S(2)}, u32[]{:S(2)}) collective-permute-start(f32[8,3,2048]{2,0,1:T(8,128)S(1)} %pad_maximum_fusion.7), channel_id=1, source_target_pairs={{1,0},{2,1},{3,2},{4,3},{5,4},{6,5},{7,6},{8,7},{9,8},{10,9},{11,1... | collective-permute-start | bytes 589832 | tf_op jit(solution)/shard_map/ppermute | solution.py:37
  9.9 23.2 %copy-start = (f32[8,32,2048]{2,1,0:T(8,128)S(1)}, f32[8,32,2048]{2,1,0:T(8,128)}, u32[]{:S(2)}) copy-start(f32[8,32,2048]{2,1,0:T(8,128)} %param.11) | copy-start | bytes 6291460
  10.9 10.9 %collective-permute-start.7 = (f32[2,3,512]{2,1,0:T(4,128)S(1)}, f32[2,3,512]{2,1,0:T(4,128)S(1)}, u32[]{:S(2)}, u32[]{:S(2)}) collective-permute-start(f32[2,3,512]{2,1,0:T(4,128)S(1)} %get-tuple-element.35), channel_id=1, source_target_pairs={{0,4},{4,8},{8,12},{12,16},{16,20},{20,24},{24,28},{1,5},{5,9},{9,... | collective-permute-start | bytes 36872 | tf_op jit(solution)/shard_map/ppermute | solution.py:37
  15.5 6.3 %collective-permute-start.8 = (f32[2,3,512]{2,1,0:T(4,128)S(1)}, f32[2,3,512]{2,1,0:T(4,128)S(1)}, u32[]{:S(2)}, u32[]{:S(2)}) collective-permute-start(f32[2,3,512]{2,1,0:T(4,128)S(1)} %get-tuple-element.36), channel_id=1, source_target_pairs={{4,0},{8,4},{12,8},{16,12},{20,16},{24,20},{28,24},{5,1},{9,5},{13... | collective-permute-start | bytes 36872 | tf_op jit(solution)/shard_map/ppermute | solution.py:37
  21.8 0.8 copy-start.6
  21.8 0.8 copy-start.7
  22.6 7.1 %collective-permute-start.10 = (f32[2,134,3]{2,1,0:T(8,128)}, f32[2,134,3]{2,1,0:T(8,128)S(1)}, u32[]{:S(2)}, u32[]{:S(2)}) collective-permute-start(f32[2,134,3]{2,1,0:T(8,128)} %get-tuple-element.34), channel_id=1, source_target_pairs={{1,0},{2,1},{3,2},{5,4},{6,5},{7,6},{9,8},{10,9},{11,10},{13,12},{... | collective-permute-start | bytes 9656 | tf_op jit(solution)/shard_map/ppermute | solution.py:37
  23.9 7.5 %collective-permute-start.9 = (f32[2,134,3]{2,1,0:T(8,128)}, f32[2,134,3]{2,1,0:T(8,128)}, u32[]{:S(2)}, u32[]{:S(2)}) collective-permute-start(f32[2,134,3]{2,1,0:T(8,128)} %get-tuple-element.33), channel_id=1, source_target_pairs={{0,1},{1,2},{2,3},{4,5},{5,6},{6,7},{8,9},{9,10},{10,11},{12,13},{... | collective-permute-start | bytes 9656 | tf_op jit(solution)/shard_map/ppermute | solution.py:37
  33.0 0.7 copy-start.11
  33.6 1.6 %copy-start.1 = (f32[8,32,2048]{2,1,0:T(8,128)S(1)}, f32[8,32,2048]{2,1,0:T(8,128)}, u32[]{:S(2)}) copy-start(f32[8,32,2048]{2,1,0:T(8,128)} %param.12) | copy-start | bytes 6291460
  33.6 1.6 %copy-start.12 = (f32[8]{0:T(128)S(1)}, f32[8]{0:T(128)}, u32[]{:S(2)}) copy-start(f32[8]{0:T(128)} %param.13) | copy-start | bytes 100
  33.6 1.6 %copy-start.16 = (pred[34]{0:T(512)(128)(4,1)S(1)}, pred[34]{0:T(512)(128)(4,1)}, u32[]{:S(2)}) copy-start(pred[34]{0:T(512)(128)(4,1)} %compare_and_fusion.2) | copy-start | bytes 106
  45.9 6.0 %collective-permute-start.2 = (f32[2,2048]{1,0:T(2,128)S(1)}, f32[2,2048]{1,0:T(2,128)S(1)}, u32[]{:S(2)}, u32[]{:S(2)}) collective-permute-start(f32[2,2048]{1,0:T(2,128)S(1)} %get-tuple-element.37), channel_id=1, source_target_pairs={{0,1},{1,2},{2,3},{3,4},{4,5},{5,6},{6,7},{7,8},{8,9},{9,10},{10,1... | collective-permute-start | bytes 49160 | tf_op jit(solution)/shard_map/ppermute | solution.py:37
  50.2 5.6 %collective-permute-start.3 = (f32[2,2048]{1,0:T(2,128)S(1)}, f32[2,2048]{1,0:T(2,128)S(1)}, u32[]{:S(2)}, u32[]{:S(2)}) collective-permute-start(f32[2,2048]{1,0:T(2,128)S(1)} %get-tuple-element.38), channel_id=1, source_target_pairs={{1,0},{2,1},{3,2},{4,3},{5,4},{6,5},{7,6},{8,7},{9,8},{10,9},{11,1... | collective-permute-start | bytes 49160 | tf_op jit(solution)/shard_map/ppermute | solution.py:37
  56.3 8.9 %collective-permute-start.4 = (f32[1,2,36,516]{3,2,1,0:T(8,128)S(1)}, f32[1,2,36,516]{3,2,1,0:T(8,128)S(1)}, u32[]{:S(2)}, u32[]{:S(2)}) collective-permute-start(f32[1,2,36,516]{3,2,1,0:T(8,128)S(1)} %get-tuple-element.26), channel_id=1, source_target_pairs={{0,1},{1,0},{2,3},{3,2},{4,5},{5,4},{6,7},{7,6},{8,9},{9,8},{10,11... | collective-permute-start | bytes 445832 | tf_op jit(solution)/shard_map/ppermute | solution.py:131
  56.4 11.5 %collective-permute-start.5 = (f32[1,2,36,516]{3,2,1,0:T(8,128)S(1)}, f32[1,2,36,516]{3,2,1,0:T(8,128)S(1)}, u32[]{:S(2)}, u32[]{:S(2)}) collective-permute-start(f32[1,2,36,516]{3,2,1,0:T(8,128)S(1)} %get-tuple-element.25), channel_id=1, source_target_pairs={{0,2},{1,3},{2,0},{3,1},{4,6},{5,7},{6,4},{7,5},{8,10},{9,11},{10,... | collective-permute-start | bytes 445832 | tf_op jit(solution)/shard_map/ppermute | solution.py:131
  60.9 10.2 %collective-permute-start.6 = (f32[1,2,36,516]{3,2,1,0:T(8,128)S(1)}, f32[1,2,36,516]{3,2,1,0:T(8,128)S(1)}, u32[]{:S(2)}, u32[]{:S(2)}) collective-permute-start(f32[1,2,36,516]{3,2,1,0:T(8,128)S(1)} %get-tuple-element.24), channel_id=1, source_target_pairs={{0,3},{1,2},{2,1},{3,0},{4,7},{5,6},{6,5},{7,4},{8,11},{9,10},{10,... | collective-permute-start | bytes 445832 | tf_op jit(solution)/shard_map/ppermute | solution.py:131
  71.1 1.3 copy-start.14
  71.1 1.3 copy-start.15
  72.1 1.1 copy-start.13
  72.1 1.1 copy-start.17
  116.9 25.1 %copy-start.4 = (f32[2,1,6144]{2,1,0:T(1,128)S(1)}, f32[2,1,6144]{2,1,0:T(1,128)}, u32[]{:S(2)}) copy-start(f32[2,1,6144]{2,1,0:T(1,128)} %param.20) | copy-start | bytes 147460
  116.9 25.1 %copy-start.9 = (f32[1,6144]{1,0:T(1,128)S(1)}, f32[1,6144]{1,0:T(1,128)}, u32[]{:S(2)}) copy-start(f32[1,6144]{1,0:T(1,128)} %param.21) | copy-start | bytes 73732
